TPU v7x, 32 devices: a whole 2x2x4 slice. The times are simulated.
32 devices in a mesh: tm: 2 (over x), prow: 4 (over z), pcol: 4 (over y, core).
Axes of the slice: x: 2, y: 2, z: 4, core: 2. Of those that a mesh axis runs over, the one named last changes fastest.
Arguments:
- signal: bfloat16 [2048, 15360], P(('prow', 'pcol'), 'tm'), may hold values from -8 to 8
- offsets: int32 [4], replicated, may hold values from 0 to 511, as said below
- pair_list: int32 [4, 4, 4, 2], P('prow', 'pcol'), may hold values from 0 to 3, as said below
Outputs:
- correlations: bfloat16 [4, 4, 4, 128, 128, 256], P('prow', 'pcol', None, 'tm')
Inputs may be any that keep to these rules, and one draw needn't show every extreme that they name: `offsets`: some window has the largest offset. `pair_list`: entry (a, b) of cell (r, c) pairs row block r n + a with column block b n + c, n the number of devices of pcol, and the row block's number is never above the column block's; pairs may repeat.
All inputs are finite; a program needn't handle non-finite values.
Results may differ from a plain program's by a relative error of at most 0.0058.
Values may be sent and summed in bfloat16 or wider, within the bound.
No kernel may reach another device: no remote copies, remote signals or barrier semaphores. Data moves between devices by JAX's collectives and lax.ppermute only.
A program may use at most 128 MiB of HBM per device.

v0:
```python
import math
import jax
import jax.numpy as jnp
from jax import lax
from jax.sharding import PartitionSpec as P

WIN = 7680
NF = 384
K0 = 32
LAGS = 256
SPAN = 4
NP = 4
STEP = 3840
HALO = 4352
two_pi = 2.0 * math.pi


def from_behind(value, axis, steps):
    count = lax.axis_size(axis)
    initial, last = (max(0, -steps), min(count, count - steps))
    return lax.ppermute(value, axis, [(source, source + steps) for source in range(initial, last)])


def forward_table():
    sample_idx = jnp.arange(WIN, dtype=jnp.int32)
    freq_bins = K0 + jnp.arange(NF, dtype=jnp.int32)
    wrapped = sample_idx[:, None] * freq_bins[None, :] % WIN
    phase_angle = wrapped.astype(jnp.float32) * (two_pi / WIN)
    taper_curve = 0.5 - 0.5 * jnp.cos(sample_idx.astype(jnp.float32) * (two_pi / WIN))
    cosine = taper_curve[:, None] * jnp.cos(phase_angle)
    sine = -taper_curve[:, None] * jnp.sin(phase_angle)
    return jnp.concatenate([cosine, sine], axis=1).astype(jnp.bfloat16)


def lag_table(count):
    freq_bins = K0 + jnp.arange(NF, dtype=jnp.int32)
    shifted = (jnp.arange(LAGS, dtype=jnp.int32) - LAGS // 2) % WIN
    wrapped = freq_bins[:, None] * shifted[None, :] % WIN
    phase_angle = wrapped.astype(jnp.float32) * (two_pi / WIN)
    factor = 1.0 / math.sqrt(NF * count)
    return jnp.concatenate(
        [jnp.cos(phase_angle) * factor, -jnp.sin(phase_angle) * factor], axis=0
    ).astype(jnp.bfloat16)


def whiten(spectra):
    real_part = spectra[..., :NF]
    imag_part = spectra[..., NF:]
    power_sum = real_part * real_part + imag_part * imag_part
    freq_bins = jnp.arange(NF, dtype=jnp.int32)
    band_matrix = (jnp.abs(freq_bins[:, None] - freq_bins[None, :]) <= SPAN).astype(jnp.float32)
    smooth = jnp.einsum(
        "...f,fg->...g", power_sum, band_matrix, precision=lax.Precision.HIGHEST
    ) / (2 * SPAN + 1)
    water_level = jnp.mean(power_sum, axis=-1, keepdims=True)
    weight = lax.rsqrt(smooth + 0.5 * water_level + 1e-06)
    return (spectra * jnp.concatenate([weight, weight], axis=-1)).astype(jnp.bfloat16)


def cross_pair(row_block, col_block, lags):
    row_real = row_block[..., :NF]
    row_imag = row_block[..., NF:]
    col_both = jnp.concatenate([col_block[..., :NF], col_block[..., NF:]], axis=0)
    row_first = jnp.concatenate([row_real, row_imag], axis=0)
    row_second = jnp.concatenate([row_imag, -row_real], axis=0)
    real_sum = jnp.einsum("wif,wjf->ijf", row_first, col_both, preferred_element_type=jnp.float32)
    imag_sum = jnp.einsum("wif,wjf->ijf", row_second, col_both, preferred_element_type=jnp.float32)
    cross = jnp.concatenate([real_sum, imag_sum], axis=-1).astype(jnp.bfloat16)
    flat = cross.reshape(-1, 2 * NF)
    result = jnp.dot(flat, lags, preferred_element_type=jnp.float32).astype(jnp.bfloat16)
    return result.reshape(row_block.shape[1], col_block.shape[1], LAGS)


def on_device(signal, offsets, pair_list):
    channels_here = signal.shape[0]
    samples_here = signal.shape[1]
    w_dev = samples_here // STEP
    n_tm = lax.axis_size("tm")
    tm_index = lax.axis_index("tm")
    dft_table = forward_table()
    head_samples = signal[:, :HALO]
    next_head = from_behind(head_samples, "tm", -1)
    extended = jnp.concatenate([signal, next_head], axis=1)

    def one_window(window):
        first_sample = window * STEP + offsets[tm_index * w_dev + window]
        segment = lax.dynamic_slice_in_dim(extended, first_sample, WIN, 1)
        return jnp.dot(segment, dft_table, preferred_element_type=jnp.float32)

    spectra = lax.map(one_window, jnp.arange(w_dev, dtype=jnp.int32))
    whitened = whiten(spectra)
    own_piece = whitened[None]
    row_gathered = lax.all_gather(own_piece, ("tm", "pcol"), axis=0, tiled=True)
    col_gathered = lax.all_gather(own_piece, ("tm", "prow"), axis=0, tiled=True)
    row_gathered = row_gathered.reshape(n_tm, -1, w_dev, channels_here, 2 * NF)
    col_gathered = col_gathered.reshape(n_tm, -1, w_dev, channels_here, 2 * NF)
    pick_dim = 1
    lags = lag_table(n_tm * w_dev)
    local_pairs = pair_list[0, 0]
    half_rows = channels_here // n_tm
    first_row = tm_index * half_rows

    def one_pair(pair_index):
        row_pick = local_pairs[pair_index, 0]
        col_pick = local_pairs[pair_index, 1]
        row_whole = lax.dynamic_index_in_dim(row_gathered, row_pick, pick_dim, keepdims=False)
        col_whole = lax.dynamic_index_in_dim(col_gathered, col_pick, pick_dim, keepdims=False)
        row_whole = row_whole.reshape(n_tm * w_dev, channels_here, 2 * NF)
        col_whole = col_whole.reshape(n_tm * w_dev, channels_here, 2 * NF)
        row_block = lax.dynamic_slice_in_dim(row_whole, first_row, half_rows, 1)
        return cross_pair(row_block, col_whole, lags)

    result = lax.map(one_pair, jnp.arange(NP, dtype=jnp.int32))
    return result.reshape(1, 1, NP, half_rows, channels_here, LAGS)


def solution(mesh):
    placed = (P(("prow", "pcol"), "tm"), P(), P("prow", "pcol", None, None))
    return jax.shard_map(
        on_device,
        mesh=mesh,
        in_specs=placed,
        out_specs=P("prow", "pcol", None, "tm", None, None),
        check_vma=False,
    )
```

profile of v0, /device:TPU:0, one launch (start us, length us, event | category | flops | bytes accessed | tf_op | source)
XLA Modules:
  0.0 409.1 jit_solution(12209533261240623052)
XLA Ops:
  6.5 1.3 slice.29
  7.9 1.3 collective-permute-start
  9.3 52.4 %multiply_convert_fusion.1 = (bf16[7680,384]{1,0:T(8,128)(2,1)S(1)}, bf16[7680,384]{1,0:T(8,128)(2,1)S(1)}) fusion(s32[384]{0:T(512)S(1)} %iota_add_fusion, f32[7680]{0:T(1024)S(1)} %get-tuple-element.245, f32[7680]{0:T(1024)S(1)} %get-tuple-element.246), kind=kLoop, calls=%fused_computation.36 | loop fusion | flops 38338560 | bytes 11859456 | tf_op jit(solution)/shard_map/convert.8
  61.8 5.0 %pad_maximum_fusion.3 = bf16[7680,768]{1,0:T(8,128)(2,1)} fusion(bf16[7680,384]{1,0:T(8,128)(2,1)S(1)} %get-tuple-element.244, bf16[7680,384]{1,0:T(8,128)(2,1)S(1)} %get-tuple-element.243), kind=kLoop, calls=%fused_computation.34 | loop fusion | flops 23592960 | bytes 23592960 | tf_op jit(solution)/shard_map/concatenate | solution.py:32
  66.7 1.4 pad_maximum_fusion.4
  68.2 19.9 %while.24 = (s32[]{:T(128)}, f32[2,128,768]{2,1,0:T(8,128)}, s32[2]{0:T(128)S(1)}, s32[]{:T(128)}, s32[4]{0:T(128)S(1)}, /*index=5*/bf16[128,12032]{1,0:T(8,128)...) while((s32[]{:T(128)}, f32[2,128,768]{2,1,0:T(8,128)}, ...), condition=%wide.region_1.2_spmd, body=%wide.region_0.1_spmd.sunk | while | flops 1509949440 | bytes 14156537 | solution.py:90
  68.2 0.6 dynamic_slice.65
  71.2 7.0 %fusion.61 = f32[2,128,768]{2,1,0:T(8,128)} fusion(f32[2,128,768]{2,1,0:T(8,128)} %get-tuple-element.370, s32[]{:T(128)} %get-tuple-element.369, bf16[7680,768]{1,0:T(8,128)(2,1)} %get-tuple-element.387, bf16[128,12032]{1,0:T(8,128)(2,1)S(1)} %get-tuple-element.386, s32[]{:T(128)S(6)} %select_n.90), kind=kOutput, calls=%fused_computation.3.clone.1 | convolution fusion | flops 1509949440 | bytes 14156292 | tf_op jit(solution)/shard_map/while/body/eval_jaxpr/dot_general | solution.py:88
  78.2 0.6 dynamic_slice.65
  81.2 6.9 %fusion.61 = f32[2,128,768]{2,1,0:T(8,128)} fusion(f32[2,128,768]{2,1,0:T(8,128)} %get-tuple-element.370, s32[]{:T(128)} %get-tuple-element.369, bf16[7680,768]{1,0:T(8,128)(2,1)} %get-tuple-element.387, bf16[128,12032]{1,0:T(8,128)(2,1)S(1)} %get-tuple-element.386, s32[]{:T(128)S(6)} %select_n.90), kind=kOutput, calls=%fused_computation.3.clone.1 | convolution fusion | flops 1509949440 | bytes 14156292 | tf_op jit(solution)/shard_map/while/body/eval_jaxpr/dot_general | solution.py:88
  88.2 1.2 fusion.42
  89.4 1.7 fusion.32
  91.1 2.0 fusion.33
  93.2 0.7 all-gather.7.cloned.1.call-update
  93.9 2.0 multiply_convert_fusion.3
  95.9 62.2 %all-gather.5.cloned.1.call-done = bf16[16,128,768]{2,1,0:T(8,128)(2,1)} async-done(((bf16[2,128,768]{2,1,0:T(8,128)(2,1)}), bf16[16,128,768]{2,1,0:T(8,128)(2,1)}) %all-gather.5.cloned.1.call-update) | async-done | bytes 3145744 | tf_op jit(solution)/shard_map/all_gather | solution.py:94
  158.1 32.8 %all-gather.7.cloned.1.call-done = bf16[16,128,768]{2,1,0:T(8,128)(2,1)} async-done(((bf16[2,128,768]{2,1,0:T(8,128)(2,1)}), bf16[16,128,768]{2,1,0:T(8,128)(2,1)}) %all-gather.7.cloned.1.call-update) | async-done | bytes 3145744 | tf_op jit(solution)/shard_map/all_gather | solution.py:93
  190.9 211.1 %while.25 = (s32[]{:T(128)}, bf16[4,64,128,256]{3,2,1,0:T(8,128)(2,1)}, s32[4]{0:T(128)S(1)}, s32[4,2]{0,1:T(2,128)S(1)}, bf16[2,4,2,128,768]{4,3,2,1,0:T(8,128)...) while((s32[]{:T(128)}, ...), condition=%wide.region_4.5_spmd, body=%wide.region_3.4_spmd.sunk | while | flops 3360456704 | bytes 74515224 | solution.py:113
  212.0 0.6 dynamic_slice.69
  214.5 0.6 constant_dynamic-slice_fusion.9
  218.7 1.5 constant_dynamic-slice_fusion.10
  220.2 0.6 copy.20
  220.8 0.6 fusion.66
  221.4 0.6 copy.21
  222.3 2.2 convolution_convert_fusion.5
  224.5 12.5 %copy.23 = bf16[48,8,64,128]{3,1,2,0:T(8,128)(2,1)S(1)} copy(bf16[48,8,64,128]{3,2,1,0:T(8,128)(2,1)S(1)} %bitcast.66) | data formatting | bytes 12582912 | tf_op jit(solution)/shard_map/while
  237.0 2.2 convolution_convert_fusion.4
  239.1 12.5 %copy.22 = bf16[48,8,64,128]{3,1,2,0:T(8,128)(2,1)S(1)} copy(bf16[48,8,64,128]{3,2,1,0:T(8,128)(2,1)S(1)} %bitcast.65) | data formatting | bytes 12582912 | tf_op jit(solution)/shard_map/while
  251.6 5.6 %fusion.68 = bf16[8192,256]{1,0:T(8,128)(2,1)S(1)} fusion(bf16[768,256]{1,0:T(8,128)(2,1)S(1)} %get-tuple-element.424, bf16[8192,384]{0,1:T(8,128)(2,1)S(1)} %bitcast.68, bf16[8192,384]{0,1:T(8,128)(2,1)S(1)} %bitcast.67), kind=kOutput, calls=%fused_computation.9.clone.1 | convolution fusion | flops 3248488448 | bytes 17170432 | tf_op jit(solution)/shard_map/while/body/eval_jaxpr/dot_general | solution.py:70
  257.2 2.3 constant_dynamic-update-slice_fusion.2
  259.5 0.6 dynamic_slice.69
  262.0 0.6 constant_dynamic-slice_fusion.9
  266.2 1.5 constant_dynamic-slice_fusion.10
  267.7 0.6 copy.20
  268.3 0.6 fusion.66
  268.9 0.6 copy.21
  269.8 2.2 convolution_convert_fusion.5
  272.0 12.5 %copy.23 = bf16[48,8,64,128]{3,1,2,0:T(8,128)(2,1)S(1)} copy(bf16[48,8,64,128]{3,2,1,0:T(8,128)(2,1)S(1)} %bitcast.66) | data formatting | bytes 12582912 | tf_op jit(solution)/shard_map/while
  284.4 2.2 convolution_convert_fusion.4
  286.6 12.5 %copy.22 = bf16[48,8,64,128]{3,1,2,0:T(8,128)(2,1)S(1)} copy(bf16[48,8,64,128]{3,2,1,0:T(8,128)(2,1)S(1)} %bitcast.65) | data formatting | bytes 12582912 | tf_op jit(solution)/shard_map/while
  299.1 5.6 %fusion.68 = bf16[8192,256]{1,0:T(8,128)(2,1)S(1)} fusion(bf16[768,256]{1,0:T(8,128)(2,1)S(1)} %get-tuple-element.424, bf16[8192,384]{0,1:T(8,128)(2,1)S(1)} %bitcast.68, bf16[8192,384]{0,1:T(8,128)(2,1)S(1)} %bitcast.67), kind=kOutput, calls=%fused_computation.9.clone.1 | convolution fusion | flops 3248488448 | bytes 17170432 | tf_op jit(solution)/shard_map/while/body/eval_jaxpr/dot_general | solution.py:70
  304.7 2.3 constant_dynamic-update-slice_fusion.2
  307.0 0.6 dynamic_slice.69
  309.5 0.6 constant_dynamic-slice_fusion.9
  313.7 1.5 constant_dynamic-slice_fusion.10
  315.2 0.6 copy.20
  316.4 0.6 copy.21
  317.3 2.2 convolution_convert_fusion.5
  319.5 12.5 %copy.23 = bf16[48,8,64,128]{3,1,2,0:T(8,128)(2,1)S(1)} copy(bf16[48,8,64,128]{3,2,1,0:T(8,128)(2,1)S(1)} %bitcast.66) | data formatting | bytes 12582912 | tf_op jit(solution)/shard_map/while
  331.9 2.2 convolution_convert_fusion.4
  334.1 12.5 %copy.22 = bf16[48,8,64,128]{3,1,2,0:T(8,128)(2,1)S(1)} copy(bf16[48,8,64,128]{3,2,1,0:T(8,128)(2,1)S(1)} %bitcast.65) | data formatting | bytes 12582912 | tf_op jit(solution)/shard_map/while
  346.6 5.6 %fusion.68 = bf16[8192,256]{1,0:T(8,128)(2,1)S(1)} fusion(bf16[768,256]{1,0:T(8,128)(2,1)S(1)} %get-tuple-element.424, bf16[8192,384]{0,1:T(8,128)(2,1)S(1)} %bitcast.68, bf16[8192,384]{0,1:T(8,128)(2,1)S(1)} %bitcast.67), kind=kOutput, calls=%fused_computation.9.clone.1 | convolution fusion | flops 3248488448 | bytes 17170432 | tf_op jit(solution)/shard_map/while/body/eval_jaxpr/dot_general | solution.py:70
  352.2 2.3 constant_dynamic-update-slice_fusion.2
  354.4 0.6 dynamic_slice.69
  357.0 0.6 constant_dynamic-slice_fusion.9
  361.2 1.5 constant_dynamic-slice_fusion.10
  362.7 0.6 copy.20
  363.9 0.6 copy.21
  364.8 2.2 convolution_convert_fusion.5
  366.9 12.5 %copy.23 = bf16[48,8,64,128]{3,1,2,0:T(8,128)(2,1)S(1)} copy(bf16[48,8,64,128]{3,2,1,0:T(8,128)(2,1)S(1)} %bitcast.66) | data formatting | bytes 12582912 | tf_op jit(solution)/shard_map/while
  379.4 2.2 convolution_convert_fusion.4
  381.6 12.5 %copy.22 = bf16[48,8,64,128]{3,1,2,0:T(8,128)(2,1)S(1)} copy(bf16[48,8,64,128]{3,2,1,0:T(8,128)(2,1)S(1)} %bitcast.65) | data formatting | bytes 12582912 | tf_op jit(solution)/shard_map/while
  394.1 5.6 %fusion.68 = bf16[8192,256]{1,0:T(8,128)(2,1)S(1)} fusion(bf16[768,256]{1,0:T(8,128)(2,1)S(1)} %get-tuple-element.424, bf16[8192,384]{0,1:T(8,128)(2,1)S(1)} %bitcast.68, bf16[8192,384]{0,1:T(8,128)(2,1)S(1)} %bitcast.67), kind=kOutput, calls=%fused_computation.9.clone.1 | convolution fusion | flops 3248488448 | bytes 17170432 | tf_op jit(solution)/shard_map/while/body/eval_jaxpr/dot_general | solution.py:70
  399.6 2.3 constant_dynamic-update-slice_fusion.2
  (27 shorter events, 3.7 us)
Async XLA Ops:
  6.5 151.5 %all-gather.5.cloned.1.call-start = ((), (), s32[]{:S(2)}) async-start(), calls=%async_computation | async-start | bytes 3538944 | tf_op jit(solution)/shard_map/all_gather | solution.py:94
  7.9 58.9 %collective-permute-start = (bf16[128,4352]{1,0:T(8,128)(2,1)S(1)}, bf16[128,4352]{1,0:T(8,128)(2,1)}, u32[]{:S(2)}, u32[]{:S(2)}) collective-permute-start(bf16[128,4352]{1,0:T(8,128)(2,1)S(1)} %slice.29), channel_id=1, source_target_pairs={{16,0},{17,1},{18,2},{19,3},{20,4},{21,5},{22,6},{23,7},{24,8},{25... | collective-permute-start | bytes 3342344 | tf_op jit(solution)/shard_map/ppermute | solution.py:21
  61.8 5.0 %copy-start = (bf16[128,7680]{1,0:T(8,128)(2,1)S(1)}, bf16[128,7680]{1,0:T(8,128)(2,1)}, u32[]{:S(2)}) copy-start(bf16[128,7680]{1,0:T(8,128)(2,1)} %param.7) | copy-start | bytes 5898244
  61.8 6.4 %copy-start.2 = (s32[4]{0:T(128)S(1)}, s32[4]{0:T(128)}, u32[]{:S(2)}) copy-start(s32[4]{0:T(128)} %param.8) | copy-start | bytes 52
  68.2 122.6 %copy-start.1 = (s32[1,1,4,2]{2,3,1,0:T(2,128)S(1)}, s32[1,1,4,2]{2,3,1,0:T(2,128)}, u32[]{:S(2)}) copy-start(s32[1,1,4,2]{2,3,1,0:T(2,128)} %param.9) | copy-start | bytes 100
  93.1 97.7 %all-gather.7.cloned.1.call-start = ((), (), s32[]{:S(2)}) async-start(), calls=%async_computation.1 | async-start | bytes 3538944 | tf_op jit(solution)/shard_map/all_gather | solution.py:93
Sparse Core Ops, SparseCore 0:
  93.2 64.8 all-gather.4
  160.0 30.8 all-gather.6
where the time goes:
time: 415 us; the launch traced here: 409 us
  local copies, waits for them, and re-layouts  130 us (31%)
  waiting for transfers between devices  95.7 us (23%)
  other arithmetic  66.6 us (16%)
  matrix products  55.2 us (13%)
  loops' own time  46.9 us (11%)
  between operations  13.9 us (3%)
    while x8, local copies, waits for them, and re-layouts  99.7 us
    all_gather x1, waiting for transfers between devices, on_device(): col_gathered = lax.all_gather(own_piece, ('tm', 'prow'), axis=0, tiled=True)  62.2 us
    another operation x2, other arithmetic  54.4 us
    another operation x1, loops' own time, on_device(): result = lax.map(one_pair, jnp.arange(NP, dtype=jnp.int32))  43.2 us
    all_gather x1, waiting for transfers between devices, on_device(): row_gathered = lax.all_gather(own_piece, ('tm', 'pcol'), axis=0, tiled=True)  32.8 us
    dot_general x4, matrix products, cross_pair(): jnp.dot(flat, lags, preferred_element_type=jnp.float32).astype(jnp.bfloat16)  22.3 us
    dot_general x2, matrix products, one_window(): return jnp.dot(segment, dft_table, preferred_element_type=jnp.float32)  13.9 us
    dynamic_update_slice x4, local copies, waits for them, and re-layouts, on_device(): result = lax.map(one_pair, jnp.arange(NP, dtype=jnp.int32))  9.16 us
  transfers between devices with their start and end apart: 3, of which 2 were waited for; matrix products, arithmetic and copies ran while one was open for 15% of the time, Pallas kernels for 0%

commit v1 on v0

--- a/solution.py
+++ b/solution.py
@@ -13,6 +13,12 @@
 STEP = 3840
 HALO = 4352
 two_pi = 2.0 * math.pi
+
+
+def joined_along(blocks, dim):
+    blocks = jnp.moveaxis(blocks, 0, dim)
+    lengths = blocks.shape
+    return blocks.reshape(*lengths[:dim], lengths[dim] * lengths[dim + 1], *lengths[dim + 2 :])
 
 
 def from_behind(value, axis, steps):
@@ -90,7 +96,19 @@
     spectra = lax.map(one_window, jnp.arange(w_dev, dtype=jnp.int32))
     whitened = whiten(spectra)
     own_piece = whitened[None]
-    row_gathered = lax.all_gather(own_piece, ("tm", "pcol"), axis=0, tiled=True)
+    peers = lax.axis_size(("tm", "pcol"))
+    pairs = [(i, (i + 1) % peers) for i in range(peers)]
+    back = [(b, a) for a, b in pairs]
+    lower, upper = ([], [])
+    for lap in range(peers - 1):
+        if lap % 2 == 0:
+            lower.append(lax.ppermute(lower[-1] if lower else own_piece, ("tm", "pcol"), pairs))
+        else:
+            upper.append(lax.ppermute(upper[-1] if upper else own_piece, ("tm", "pcol"), back))
+    tiles = jnp.stack([*lower[::-1], own_piece, *upper])
+    shift = lax.axis_index(("tm", "pcol")) - len(lower)
+    tiles = tiles[(jnp.arange(peers) - shift) % peers]
+    row_gathered = joined_along(tiles, 0)
     col_gathered = lax.all_gather(own_piece, ("tm", "prow"), axis=0, tiled=True)
     row_gathered = row_gathered.reshape(n_tm, -1, w_dev, channels_here, 2 * NF)
     col_gathered = col_gathered.reshape(n_tm, -1, w_dev, channels_here, 2 * NF)

time: 415 us -> 390 us (0.940)
  waiting for transfers between devices: 95.7 us -> 48.9 us
  local copies, waits for them, and re-layouts: 130 us -> 140 us
  starting transfers between devices: 1.34 us -> 9.88 us
    all_gather x1, waiting for transfers between devices: 62.2 us -> 15.7 us  [on_device(): col_gathered = lax.all_gather(own_piece, ('tm', 'prow'), axis=0, tiled=True)]
    ppermute x0 -> x7, waiting for transfers between devices: none -> 33.2 us  [the longest x4 33.2 us: on_device(): lax.ppermute(lower[-1] if lower else own_piece, ('tm', 'pcol'), pairs)]
    all_gather x1 -> x0, waiting for transfers between devices: 32.8 us -> none  [on_device(): row_gathered = lax.all_gather(own_piece, ('tm', 'pcol'), axis=0, tiled=True)]
    ppermute x0 -> x7, starting transfers between devices: none -> 8.58 us  [the longest x3 8.03 us: on_device(): lax.ppermute(upper[-1] if upper else own_piece, ('tm', 'pcol'), back)]
    unnamed x6 -> x21, local copies, waits for them, and re-layouts: 0.02 us -> 7.95 us
  transfers between devices with their start and end apart: 3 -> 9, of which waited for: 2 -> 5; matrix products, arithmetic and copies ran while one was open for 15% -> 18% of each run, Pallas kernels for 0% -> 0%
where the time goes in v1:
time: 390 us; the launch traced here: 383 us
  local copies, waits for them, and re-layouts  140 us (36%)
  other arithmetic  66.6 us (17%)
  matrix products  55.1 us (14%)
  waiting for transfers between devices  48.9 us (13%)
  loops' own time  48.2 us (12%)
  between operations  14 us (4%)
  starting transfers between devices  9.88 us (3%)
    while x8, local copies, waits for them, and re-layouts  99.7 us
    another operation x2, other arithmetic  54.4 us
    another operation x1, loops' own time, on_device(): result = lax.map(one_pair, jnp.arange(NP, dtype=jnp.int32))  44.2 us
    ppermute x4, waiting for transfers between devices, on_device(): lax.ppermute(lower[-1] if lower else own_piece, ('tm', 'pcol'), pairs)  33.2 us
    dot_general x4, matrix products, cross_pair(): jnp.dot(flat, lags, preferred_element_type=jnp.float32).astype(jnp.bfloat16)  22.2 us
    all_gather x1, waiting for transfers between devices, on_device(): col_gathered = lax.all_gather(own_piece, ('tm', 'prow'), axis=0, tiled=True)  15.7 us
    dot_general x2, matrix products, one_window(): return jnp.dot(segment, dft_table, preferred_element_type=jnp.float32)  13.9 us
    dynamic_update_slice x4, local copies, waits for them, and re-layouts, on_device(): result = lax.map(one_pair, jnp.arange(NP, dtype=jnp.int32))  9.16 us
  transfers between devices with their start and end apart: 9, of which 5 were waited for; matrix products, arithmetic and copies ran while one was open for 18% of the time, Pallas kernels for 0%

profile of v1, /device:TPU:0, one launch (start us, length us, event | category | flops | bytes accessed | tf_op | source)
XLA Modules:
  0.0 382.6 jit_solution(3329999451369405715)
XLA Ops:
  6.5 1.3 slice.29
  7.9 1.3 collective-permute-start
  9.3 52.4 %multiply_convert_fusion.1 = (bf16[7680,384]{1,0:T(8,128)(2,1)S(1)}, bf16[7680,384]{1,0:T(8,128)(2,1)S(1)}) fusion(s32[384]{0:T(512)S(1)} %iota_add_fusion, f32[7680]{0:T(1024)S(1)} %get-tuple-element.245, f32[7680]{0:T(1024)S(1)} %get-tuple-element.246), kind=kLoop, calls=%fused_computation.37 | loop fusion | flops 38338560 | bytes 11859456 | tf_op jit(solution)/shard_map/convert.8
  61.8 5.0 %pad_maximum_fusion.3 = bf16[7680,768]{1,0:T(8,128)(2,1)} fusion(bf16[7680,384]{1,0:T(8,128)(2,1)S(1)} %get-tuple-element.244, bf16[7680,384]{1,0:T(8,128)(2,1)S(1)} %get-tuple-element.243), kind=kLoop, calls=%fused_computation.35 | loop fusion | flops 23592960 | bytes 23592960 | tf_op jit(solution)/shard_map/concatenate | solution.py:38
  66.7 1.5 pad_maximum_fusion.4
  68.2 20.4 %while.24 = (s32[]{:T(128)}, f32[2,128,768]{2,1,0:T(8,128)}, s32[2]{0:T(128)S(1)}, s32[]{:T(128)}, s32[4]{0:T(128)S(1)}, /*index=5*/bf16[128,12032]{1,0:T(8,128)...) while((s32[]{:T(128)}, f32[2,128,768]{2,1,0:T(8,128)}, ...), condition=%wide.region_1.2_spmd, body=%wide.region_0.1_spmd.sunk | while | flops 1509949440 | bytes 14156537 | solution.py:96
  69.5 0.7 dynamic_slice.66
  71.4 7.0 %fusion.63 = f32[2,128,768]{2,1,0:T(8,128)} fusion(f32[2,128,768]{2,1,0:T(8,128)} %get-tuple-element.370, s32[]{:T(128)} %get-tuple-element.369, bf16[7680,768]{1,0:T(8,128)(2,1)} %get-tuple-element.387, bf16[128,12032]{1,0:T(8,128)(2,1)S(1)} %get-tuple-element.386, s32[]{:T(128)S(6)} %select_n.123), kind=kOutput, calls=%fused_computation.4.clone.1 | convolution fusion | flops 1509949440 | bytes 14156292 | tf_op jit(solution)/shard_map/while/body/eval_jaxpr/dot_general | solution.py:94
  79.6 0.7 dynamic_slice.66
  81.6 7.0 %fusion.63 = f32[2,128,768]{2,1,0:T(8,128)} fusion(f32[2,128,768]{2,1,0:T(8,128)} %get-tuple-element.370, s32[]{:T(128)} %get-tuple-element.369, bf16[7680,768]{1,0:T(8,128)(2,1)} %get-tuple-element.387, bf16[128,12032]{1,0:T(8,128)(2,1)S(1)} %get-tuple-element.386, s32[]{:T(128)S(6)} %select_n.123), kind=kOutput, calls=%fused_computation.4.clone.1 | convolution fusion | flops 1509949440 | bytes 14156292 | tf_op jit(solution)/shard_map/while/body/eval_jaxpr/dot_general | solution.py:94
  88.6 1.2 fusion.42
  89.9 1.7 fusion.32
  91.5 2.0 fusion.33
  94.1 10.4 %collective-permute-done.1 = bf16[1,2,128,768]{3,2,1,0:T(8,128)(2,1)S(1)} collective-permute-done((bf16[1,2,128,768]{3,2,1,0:T(8,128)(2,1)}, bf16[1,2,128,768]{3,2,1,0:T(8,128)(2,1)S(1)}, u32[]{:S(2)}, u32[]{:S(2)}) %collective-permute-start.1) | collective-permute-done | bytes 393248 | tf_op jit(solution)/shard_map/ppermute | solution.py:105
  104.4 0.7 copy-done.1
  105.2 2.6 collective-permute-start.5
  107.8 9.7 %collective-permute-done.2 = bf16[1,2,128,768]{3,2,1,0:T(8,128)(2,1)S(1)} collective-permute-done((bf16[1,2,128,768]{3,2,1,0:T(8,128)(2,1)S(1)}, bf16[1,2,128,768]{3,2,1,0:T(8,128)(2,1)S(1)}, u32[]{:S(2)}, u32[]{:S(2)}) %collective-permute-start.2) | collective-permute-done | bytes 393248 | tf_op jit(solution)/shard_map/ppermute | solution.py:105
  117.6 2.7 collective-permute-start.6
  120.3 5.5 %collective-permute-done.3 = bf16[1,2,128,768]{3,2,1,0:T(8,128)(2,1)S(1)} collective-permute-done((bf16[1,2,128,768]{3,2,1,0:T(8,128)(2,1)S(1)}, bf16[1,2,128,768]{3,2,1,0:T(8,128)(2,1)S(1)}, u32[]{:S(2)}, u32[]{:S(2)}) %collective-permute-start.3) | collective-permute-done | bytes 393248 | tf_op jit(solution)/shard_map/ppermute | solution.py:105
  125.8 2.0 multiply_convert_fusion.3
  127.8 2.7 collective-permute-start.7
  130.5 7.7 %collective-permute-done.4 = bf16[1,2,128,768]{3,2,1,0:T(8,128)(2,1)} collective-permute-done((bf16[1,2,128,768]{3,2,1,0:T(8,128)(2,1)S(1)}, bf16[1,2,128,768]{3,2,1,0:T(8,128)(2,1)}, u32[]{:S(2)}, u32[]{:S(2)}) %collective-permute-start.4) | collective-permute-done | bytes 393248 | tf_op jit(solution)/shard_map/ppermute | solution.py:105
  138.1 1.0 bitcast_dynamic-update-slice_fusion.7
  139.2 1.0 bitcast_dynamic-update-slice_fusion.6
  140.2 1.0 bitcast_dynamic-update-slice_fusion.5
  141.2 1.0 bitcast_dynamic-update-slice_fusion.4
  142.3 1.0 bitcast_dynamic-update-slice_fusion.3
  143.3 1.0 bitcast_dynamic-update-slice_fusion.2
  144.3 1.0 bitcast_dynamic-update-slice_fusion.1
  145.4 2.4 gather_fusion
  147.8 15.7 %all-gather.3.cloned.1.call-done = bf16[16,128,768]{2,1,0:T(8,128)(2,1)} async-done(((bf16[2,128,768]{2,1,0:T(8,128)(2,1)}), bf16[16,128,768]{2,1,0:T(8,128)(2,1)}) %all-gather.3.cloned.1.call-update) | async-done | bytes 3145744 | tf_op jit(solution)/shard_map/all_gather | solution.py:112
  163.6 211.8 %while.25 = (s32[]{:T(128)}, bf16[4,64,128,256]{3,2,1,0:T(8,128)(2,1)}, s32[4]{0:T(128)S(1)}, s32[4,2]{0,1:T(2,128)S(1)}, bf16[2,4,2,128,768]{4,3,2,1,0:T(8,128)...) while((s32[]{:T(128)}, ...), condition=%wide.region_4.5_spmd, body=%wide.region_3.4_spmd.sunk | while | flops 3360456704 | bytes 74515224 | solution.py:131
  187.2 0.6 constant_dynamic-slice_fusion.9
  191.6 1.5 constant_dynamic-slice_fusion.10
  195.2 2.2 convolution_convert_fusion.5
  197.4 12.5 %copy.23 = bf16[48,8,64,128]{3,1,2,0:T(8,128)(2,1)S(1)} copy(bf16[48,8,64,128]{3,2,1,0:T(8,128)(2,1)S(1)} %bitcast.86) | data formatting | bytes 12582912 | tf_op jit(solution)/shard_map/while
  209.9 2.2 convolution_convert_fusion.4
  212.0 12.5 %copy.22 = bf16[48,8,64,128]{3,1,2,0:T(8,128)(2,1)S(1)} copy(bf16[48,8,64,128]{3,2,1,0:T(8,128)(2,1)S(1)} %bitcast.85) | data formatting | bytes 12582912 | tf_op jit(solution)/shard_map/while
  224.5 5.6 %fusion.70 = bf16[8192,256]{1,0:T(8,128)(2,1)S(1)} fusion(bf16[768,256]{1,0:T(8,128)(2,1)S(1)} %get-tuple-element.424, bf16[8192,384]{0,1:T(8,128)(2,1)S(1)} %bitcast.88, bf16[8192,384]{0,1:T(8,128)(2,1)S(1)} %bitcast.87), kind=kOutput, calls=%fused_computation.10.clone.1 | convolution fusion | flops 3248488448 | bytes 17170432 | tf_op jit(solution)/shard_map/while/body/eval_jaxpr/dot_general | solution.py:76
  230.1 2.3 constant_dynamic-update-slice_fusion.2
  234.9 0.6 constant_dynamic-slice_fusion.9
  239.3 1.5 constant_dynamic-slice_fusion.10
  242.9 2.2 convolution_convert_fusion.5
  245.1 12.5 %copy.23 = bf16[48,8,64,128]{3,1,2,0:T(8,128)(2,1)S(1)} copy(bf16[48,8,64,128]{3,2,1,0:T(8,128)(2,1)S(1)} %bitcast.86) | data formatting | bytes 12582912 | tf_op jit(solution)/shard_map/while
  257.6 2.2 convolution_convert_fusion.4
  259.7 12.5 %copy.22 = bf16[48,8,64,128]{3,1,2,0:T(8,128)(2,1)S(1)} copy(bf16[48,8,64,128]{3,2,1,0:T(8,128)(2,1)S(1)} %bitcast.85) | data formatting | bytes 12582912 | tf_op jit(solution)/shard_map/while
  272.2 5.6 %fusion.70 = bf16[8192,256]{1,0:T(8,128)(2,1)S(1)} fusion(bf16[768,256]{1,0:T(8,128)(2,1)S(1)} %get-tuple-element.424, bf16[8192,384]{0,1:T(8,128)(2,1)S(1)} %bitcast.88, bf16[8192,384]{0,1:T(8,128)(2,1)S(1)} %bitcast.87), kind=kOutput, calls=%fused_computation.10.clone.1 | convolution fusion | flops 3248488448 | bytes 17170432 | tf_op jit(solution)/shard_map/while/body/eval_jaxpr/dot_general | solution.py:76
  277.8 2.3 constant_dynamic-update-slice_fusion.2
  282.6 0.6 constant_dynamic-slice_fusion.9
  287.0 1.5 constant_dynamic-slice_fusion.10
  290.6 2.2 convolution_convert_fusion.5
  292.8 12.5 %copy.23 = bf16[48,8,64,128]{3,1,2,0:T(8,128)(2,1)S(1)} copy(bf16[48,8,64,128]{3,2,1,0:T(8,128)(2,1)S(1)} %bitcast.86) | data formatting | bytes 12582912 | tf_op jit(solution)/shard_map/while
  305.2 2.2 convolution_convert_fusion.4
  307.4 12.5 %copy.22 = bf16[48,8,64,128]{3,1,2,0:T(8,128)(2,1)S(1)} copy(bf16[48,8,64,128]{3,2,1,0:T(8,128)(2,1)S(1)} %bitcast.85) | data formatting | bytes 12582912 | tf_op jit(solution)/shard_map/while
  319.9 5.6 %fusion.70 = bf16[8192,256]{1,0:T(8,128)(2,1)S(1)} fusion(bf16[768,256]{1,0:T(8,128)(2,1)S(1)} %get-tuple-element.424, bf16[8192,384]{0,1:T(8,128)(2,1)S(1)} %bitcast.88, bf16[8192,384]{0,1:T(8,128)(2,1)S(1)} %bitcast.87), kind=kOutput, calls=%fused_computation.10.clone.1 | convolution fusion | flops 3248488448 | bytes 17170432 | tf_op jit(solution)/shard_map/while/body/eval_jaxpr/dot_general | solution.py:76
  325.4 2.3 constant_dynamic-update-slice_fusion.2
  330.2 0.6 constant_dynamic-slice_fusion.9
  334.7 1.5 constant_dynamic-slice_fusion.10
  338.3 2.2 convolution_convert_fusion.5
  340.4 12.5 %copy.23 = bf16[48,8,64,128]{3,1,2,0:T(8,128)(2,1)S(1)} copy(bf16[48,8,64,128]{3,2,1,0:T(8,128)(2,1)S(1)} %bitcast.86) | data formatting | bytes 12582912 | tf_op jit(solution)/shard_map/while
  352.9 2.2 convolution_convert_fusion.4
  355.1 12.5 %copy.22 = bf16[48,8,64,128]{3,1,2,0:T(8,128)(2,1)S(1)} copy(bf16[48,8,64,128]{3,2,1,0:T(8,128)(2,1)S(1)} %bitcast.85) | data formatting | bytes 12582912 | tf_op jit(solution)/shard_map/while
  367.5 5.6 %fusion.70 = bf16[8192,256]{1,0:T(8,128)(2,1)S(1)} fusion(bf16[768,256]{1,0:T(8,128)(2,1)S(1)} %get-tuple-element.424, bf16[8192,384]{0,1:T(8,128)(2,1)S(1)} %bitcast.88, bf16[8192,384]{0,1:T(8,128)(2,1)S(1)} %bitcast.87), kind=kOutput, calls=%fused_computation.10.clone.1 | convolution fusion | flops 3248488448 | bytes 17170432 | tf_op jit(solution)/shard_map/while/body/eval_jaxpr/dot_general | solution.py:76
  373.1 2.3 constant_dynamic-update-slice_fusion.2
  (57 shorter events, 12.7 us)
Async XLA Ops:
  6.5 157.0 %all-gather.3.cloned.1.call-start = ((), (), s32[]{:S(2)}) async-start(), calls=%async_computation | async-start | bytes 3538944 | tf_op jit(solution)/shard_map/all_gather | solution.py:112
  7.9 58.9 %collective-permute-start = (bf16[128,4352]{1,0:T(8,128)(2,1)S(1)}, bf16[128,4352]{1,0:T(8,128)(2,1)}, u32[]{:S(2)}, u32[]{:S(2)}) collective-permute-start(bf16[128,4352]{1,0:T(8,128)(2,1)S(1)} %slice.29), channel_id=1, source_target_pairs={{16,0},{17,1},{18,2},{19,3},{20,4},{21,5},{22,6},{23,7},{24,8},{25... | collective-permute-start | bytes 3342344 | tf_op jit(solution)/shard_map/ppermute | solution.py:27
  61.8 5.0 %copy-start = (bf16[128,7680]{1,0:T(8,128)(2,1)S(1)}, bf16[128,7680]{1,0:T(8,128)(2,1)}, u32[]{:S(2)}) copy-start(bf16[128,7680]{1,0:T(8,128)(2,1)} %param.7) | copy-start | bytes 5898244
  66.7 1.5 copy-start.6
  93.5 10.9 %collective-permute-start.1 = (bf16[1,2,128,768]{3,2,1,0:T(8,128)(2,1)}, bf16[1,2,128,768]{3,2,1,0:T(8,128)(2,1)S(1)}, u32[]{:S(2)}, u32[]{:S(2)}) collective-permute-start(bf16[1,2,128,768]{3,2,1,0:T(8,128)(2,1)} %bitcast.95), channel_id=1, source_target_pairs={{0,1},{1,2},{2,3},{3,16},{16,17},{17,18},{18,19},{19,0},{4,5},{5,6... | collective-permute-start | bytes 1179656 | tf_op jit(solution)/shard_map/ppermute | solution.py:105
  104.4 0.7 copy-start.1
  105.2 12.4 %collective-permute-start.2 = (bf16[1,2,128,768]{3,2,1,0:T(8,128)(2,1)S(1)}, bf16[1,2,128,768]{3,2,1,0:T(8,128)(2,1)S(1)}, u32[]{:S(2)}, u32[]{:S(2)}) collective-permute-start(bf16[1,2,128,768]{3,2,1,0:T(8,128)(2,1)S(1)} %collective-permute-done.1), channel_id=1, source_target_pairs={{0,1},{1,2},{2,3},{3,16},{16,17},{17,18},{18,19},{19,0},{4,5},{5,6... | collective-permute-start | bytes 1179656 | tf_op jit(solution)/shard_map/ppermute | solution.py:105
  105.2 12.4 %collective-permute-start.5 = (bf16[1,2,128,768]{3,2,1,0:T(8,128)(2,1)}, bf16[1,2,128,768]{3,2,1,0:T(8,128)(2,1)S(1)}, u32[]{:S(2)}, u32[]{:S(2)}) collective-permute-start(bf16[1,2,128,768]{3,2,1,0:T(8,128)(2,1)} %bitcast.96), channel_id=1, source_target_pairs={{1,0},{2,1},{3,2},{16,3},{17,16},{18,17},{19,18},{0,19},{5,4},{6,5... | collective-permute-start | bytes 1179656 | tf_op jit(solution)/shard_map/ppermute | solution.py:107
  117.5 12.9 %copy-start.3 = (bf16[1,2,128,768]{3,2,1,0:T(8,128)(2,1)}, bf16[1,2,128,768]{3,2,1,0:T(8,128)(2,1)S(1)}, u32[]{:S(2)}) copy-start(bf16[1,2,128,768]{3,2,1,0:T(8,128)(2,1)S(1)} %collective-permute-done.2) | copy-start | bytes 1179652
  117.5 8.2 %collective-permute-start.3 = (bf16[1,2,128,768]{3,2,1,0:T(8,128)(2,1)S(1)}, bf16[1,2,128,768]{3,2,1,0:T(8,128)(2,1)S(1)}, u32[]{:S(2)}, u32[]{:S(2)}) collective-permute-start(bf16[1,2,128,768]{3,2,1,0:T(8,128)(2,1)S(1)} %collective-permute-done.2), channel_id=1, source_target_pairs={{0,1},{1,2},{2,3},{3,16},{16,17},{17,18},{18,19},{19,0},{4,5},{5,6... | collective-permute-start | bytes 1179656 | tf_op jit(solution)/shard_map/ppermute | solution.py:105
  117.6 12.9 %copy-start.2 = (bf16[1,2,128,768]{3,2,1,0:T(8,128)(2,1)}, bf16[1,2,128,768]{3,2,1,0:T(8,128)(2,1)S(1)}, u32[]{:S(2)}) copy-start(bf16[1,2,128,768]{3,2,1,0:T(8,128)(2,1)S(1)} %collective-permute-done.5) | copy-start | bytes 1179652
  117.6 10.2 %collective-permute-start.6 = (bf16[1,2,128,768]{3,2,1,0:T(8,128)(2,1)S(1)}, bf16[1,2,128,768]{3,2,1,0:T(8,128)(2,1)}, u32[]{:S(2)}, u32[]{:S(2)}) collective-permute-start(bf16[1,2,128,768]{3,2,1,0:T(8,128)(2,1)S(1)} %collective-permute-done.5), channel_id=1, source_target_pairs={{1,0},{2,1},{3,2},{16,3},{17,16},{18,17},{19,18},{0,19},{5,4},{6,5... | collective-permute-start | bytes 1179656 | tf_op jit(solution)/shard_map/ppermute | solution.py:107
  125.8 4.7 %copy-start.4 = (bf16[1,2,128,768]{3,2,1,0:T(8,128)(2,1)}, bf16[1,2,128,768]{3,2,1,0:T(8,128)(2,1)S(1)}, u32[]{:S(2)}) copy-start(bf16[1,2,128,768]{3,2,1,0:T(8,128)(2,1)S(1)} %collective-permute-done.3) | copy-start | bytes 1179652
  125.8 12.4 %collective-permute-start.4 = (bf16[1,2,128,768]{3,2,1,0:T(8,128)(2,1)S(1)}, bf16[1,2,128,768]{3,2,1,0:T(8,128)(2,1)}, u32[]{:S(2)}, u32[]{:S(2)}) collective-permute-start(bf16[1,2,128,768]{3,2,1,0:T(8,128)(2,1)S(1)} %collective-permute-done.3), channel_id=1, source_target_pairs={{0,1},{1,2},{2,3},{3,16},{16,17},{17,18},{18,19},{19,0},{4,5},{5,6... | collective-permute-start | bytes 1179656 | tf_op jit(solution)/shard_map/ppermute | solution.py:105
  127.8 17.6 %collective-permute-start.7 = (bf16[1,2,128,768]{3,2,1,0:T(8,128)(2,1)}, bf16[1,2,128,768]{3,2,1,0:T(8,128)(2,1)S(1)}, u32[]{:S(2)}, u32[]{:S(2)}) collective-permute-start(bf16[1,2,128,768]{3,2,1,0:T(8,128)(2,1)} %collective-permute-done.6), channel_id=1, source_target_pairs={{1,0},{2,1},{3,2},{16,3},{17,16},{18,17},{19,18},{0,19},{5,4},{6,5... | collective-permute-start | bytes 1179656 | tf_op jit(solution)/shard_map/ppermute | solution.py:107
  139.2 24.4 %copy-start.5 = (s32[1,1,4,2]{2,3,1,0:T(2,128)S(1)}, s32[1,1,4,2]{2,3,1,0:T(2,128)}, u32[]{:S(2)}) copy-start(s32[1,1,4,2]{2,3,1,0:T(2,128)} %param.9) | copy-start | bytes 100
Sparse Core Ops, SparseCore 0:
  93.7 69.8 all-gather.2
